TPU v7x, 32 devices: a whole 2x2x4 slice. The times are simulated.
32 devices in a mesh: tm: 8 (over z, y), cal: 4 (over x, core).
Axes of the slice: x: 2, y: 2, z: 4, core: 2. Of those that a mesh axis runs over, the one named last changes fastest.
Arguments:
- src_design: float32 [5, 4096, 128], P(None, ('tm', 'cal')), may hold values from -6 to 6
- att_design: float32 [3, 4096, 128], P(None, ('tm', 'cal')), may hold values from -6 to 6
- obs_phase: float32 [4096, 128], P(('tm', 'cal')), may hold values from 0 to 1
- cal_design: float32 [4096, 128], P(('tm', 'cal')), may hold values from -6 to 6
- obs_weight: float32 [4096, 128], P(('tm', 'cal')), may hold values from 0.1 to 12
- knot_index: int32 [4096, 128], P(('tm', 'cal')), may hold values from 0 to 4092, as said below
- cal_block: int32 [4096, 128], P(('tm', 'cal')), may hold values from 0 to 7
- cal_column: int32 [4096, 128], P(('tm', 'cal')), may hold values from 0 to 4095
- obs_count: int32 [4096], P(('tm', 'cal')), may hold values from 32 to 128
- src_res: float32 [5, 4096], P(None, ('tm', 'cal')), may hold values from -6 to 6
- att_res: float32 [3, 4096], P(None, ('tm', 'cal')), may hold values from -6 to 6
- cal_res: float32 [8, 4096], P('cal'), may hold values from -6 to 6
- src_dir: float32 [5, 4096], P(None, ('tm', 'cal')), may hold values from -6 to 6
- att_dir: float32 [3, 4096], P(None, ('tm', 'cal')), may hold values from -6 to 6
- cal_dir: float32 [8, 4096], P('cal'), may hold values from -6 to 6
Outputs:
- new_src_res: float32 [5, 4096], P(None, ('tm', 'cal'))
- new_att_res: float32 [3, 4096], P(None, ('tm', 'cal'))
- new_cal_res: float32 [8, 4096], P('cal')
- new_src_dir: float32 [5, 4096], P(None, ('tm', 'cal'))
- new_att_dir: float32 [3, 4096], P(None, ('tm', 'cal'))
- new_cal_dir: float32 [8, 4096], P('cal')
Inputs may be any that keep to these rules, and one draw needn't show every extreme that they name: The observations of source row s have knot intervals from (s // 128) * 128 to (s // 128) * 128 + 127, and knot_index + 3 < 4096.
All inputs are finite; a program needn't handle non-finite values.
Results may differ from a plain program's by a relative error of at most 0.00015.
Values sent between devices are 32-bit elements; how exact they have to be, the bound alone decides.
No kernel may reach another device: no remote copies, remote signals or barrier semaphores. Data moves between devices by JAX's collectives and lax.ppermute only.
A program may use at most 64 MiB of HBM per device.

v0:
```python
import math
import jax
import jax.numpy as jnp
from jax import lax
from jax.sharding import PartitionSpec as P


def passed_along(block, axis, distance):
    devices = range(lax.axis_size(axis))
    route = [(i - distance, i) for i in devices if i - distance in devices]
    return lax.ppermute(block, axis, route)


def spline(phase):
    rest = 1.0 - phase
    cube = phase * phase * phase
    square = phase * phase
    first = rest * rest * rest / 6.0
    second = (3.0 * cube - 6.0 * square + 4.0) / 6.0
    third = (-3.0 * cube + 3.0 * square + 3.0 * phase + 1.0) / 6.0
    fourth = cube / 6.0
    return (first, second, third, fourth)


def local(
    src_design,
    att_design,
    obs_phase,
    cal_design,
    obs_weight,
    knot_index,
    cal_block,
    cal_column,
    obs_count,
    src_res,
    att_res,
    cal_res,
    src_dir,
    att_dir,
    cal_dir,
):
    knot_count = att_dir.shape[1]
    extended = knot_count + 3
    blocks, col_width = cal_dir.shape
    all_blocks = blocks * lax.axis_size("cal")
    src_rows, slots = obs_phase.shape
    group = math.gcd(src_rows, 16)
    group_count = src_rows // group
    first_row = (lax.axis_index("tm") == 0).astype(jnp.float32)
    cal_values = lax.all_gather(cal_dir, "cal", axis=0, tiled=True)
    edge_knots = passed_along(att_dir[:, :3], ("tm", "cal"), -1)
    att_ext = jnp.concatenate([att_dir, edge_knots], axis=1)
    live_mask = (lax.broadcasted_iota(jnp.int32, obs_phase.shape, 1) < obs_count[:, None]).astype(
        jnp.float32
    )
    local_knot = knot_index - lax.axis_index(("tm", "cal")) * knot_count
    knot_iota = lax.broadcasted_iota(jnp.int32, (1, 1, extended), 2)

    def block_inputs(which):
        start = which * group
        knots = lax.dynamic_slice_in_dim(local_knot, start, group, 0)
        design = lax.dynamic_slice_in_dim(att_design, start, group, 1)
        phases = lax.dynamic_slice_in_dim(obs_phase, start, group, 0)
        return (start, knots, design, spline(phases))

    def forward(which):
        start, knots, design, weights = block_inputs(which)
        total = jnp.zeros((group, slots), jnp.float32)
        for offset in range(4):
            onehot = ((knots + offset)[:, :, None] == knot_iota).astype(jnp.float32)
            picked = jnp.einsum("bok,ck->cbo", onehot, att_ext, precision=lax.Precision.HIGHEST)
            total = total + weights[offset] * jnp.sum(design * picked, axis=0)
        return total

    y_att = lax.map(forward, jnp.arange(group_count, dtype=jnp.int32)).reshape(src_rows, slots)
    y_src = jnp.sum(src_design * src_dir[:, :, None], axis=0)
    flat_index = cal_block * col_width + cal_column
    y_cal = cal_design * jnp.take(cal_values.reshape(-1), flat_index)
    response = live_mask * (y_src + y_att + y_cal)
    weighted = obs_weight * response
    curv_local = jnp.sum(weighted * response)
    norm_local = (
        jnp.sum(src_res * src_res)
        + jnp.sum(att_res * att_res)
        + first_row * jnp.sum(cal_res * cal_res)
    )
    cal_term = jax.ops.segment_sum(
        (cal_design * weighted).reshape(-1),
        flat_index.reshape(-1),
        num_segments=all_blocks * col_width,
    ).reshape(all_blocks, col_width)
    q_src = jnp.sum(src_design * weighted[None], axis=2)

    def backward(which, grad_sum):
        start, knots, design, weights = block_inputs(which)
        scaled = design * lax.dynamic_slice_in_dim(weighted, start, group, 0)[None]
        for offset in range(4):
            onehot = ((knots + offset)[:, :, None] == knot_iota).astype(jnp.float32)
            grad_sum = grad_sum + jnp.einsum(
                "cbo,bok->ck",
                weights[offset][None] * scaled,
                onehot,
                precision=lax.Precision.HIGHEST,
            )
        return grad_sum

    grad_ext = lax.fori_loop(0, group_count, backward, jnp.zeros((3, extended), jnp.float32))
    incoming = passed_along(grad_ext[:, knot_count:], ("tm", "cal"), 1)
    q_att = jnp.concatenate([grad_ext[:, :3] + incoming, grad_ext[:, 3:knot_count]], axis=1)
    norm_now, curvature = lax.psum((norm_local, curv_local), ("tm", "cal"))
    shared = lax.psum_scatter(cal_term, "cal", scatter_dimension=0, tiled=True)
    q_cal = lax.psum(shared, "tm")
    step_len = norm_now / curvature
    new_src_res = src_res - step_len * q_src
    new_att_res = att_res - step_len * q_att
    new_cal_res = cal_res - step_len * q_cal
    next_local = (
        jnp.sum(new_src_res * new_src_res)
        + jnp.sum(new_att_res * new_att_res)
        + first_row * jnp.sum(new_cal_res * new_cal_res)
    )
    norm_next = lax.psum(next_local, ("tm", "cal"))
    ratio = norm_next / norm_now
    return (
        new_src_res,
        new_att_res,
        new_cal_res,
        new_src_res + ratio * src_dir,
        new_att_res + ratio * att_dir,
        new_cal_res + ratio * cal_dir,
    )


def solution(mesh):
    return jax.shard_map(
        local,
        mesh=mesh,
        in_specs=(
            P(None, ("tm", "cal"), None),
            P(None, ("tm", "cal"), None),
            P(("tm", "cal"), None),
            P(("tm", "cal"), None),
            P(("tm", "cal"), None),
            P(("tm", "cal"), None),
            P(("tm", "cal"), None),
            P(("tm", "cal"), None),
            P(("tm", "cal")),
            P(None, ("tm", "cal")),
            P(None, ("tm", "cal")),
            P("cal", None),
            P(None, ("tm", "cal")),
            P(None, ("tm", "cal")),
            P("cal", None),
        ),
        out_specs=(
            P(None, ("tm", "cal")),
            P(None, ("tm", "cal")),
            P("cal", None),
            P(None, ("tm", "cal")),
            P(None, ("tm", "cal")),
            P("cal", None),
        ),
        check_vma=False,
    )
```

profile of v0, /device:TPU:14, one launch (start us, length us, event | category | flops | bytes accessed | tf_op | source)
XLA Modules:
  0.0 395.8 jit_solution(5462069088811584754)
XLA Ops:
  7.2 1.9 collective-permute-start
  9.2 0.9 bitcast_clamp_fusion
  10.1 0.9 fusion.84
  11.0 5.4 %all-gather = f32[4,2,4096]{2,1,0:T(2,128)S(1)} all-gather(f32[1,2,4096]{2,1,0:T(2,128)S(1)} %bitcast.109), channel_id=1, replica_groups=mesh['tm'=8,'cal'=4] {'cal'}, dimensions={0}, use_global_device_ids=true | all-gather | bytes 163840 | tf_op jit(solution)/shard_map/all_gather | solution.py:50
  18.3 0.6 multiply_reduce_fusion.4
  19.0 90.5 %gather_fusion = f32[16384]{0:T(1024)S(1)} fusion(f32[32768]{0:T(1024)S(1)} %bitcast.107, s32[16384]{0:T(1024)S(1)} %bitcast_clamp_fusion), kind=kCustom, calls=%fused_computation | custom fusion | bytes 196608 | tf_op jit(solution)/shard_map/jit(_take)/gather | solution.py:78
  109.7 0.6 copy-done.9
  113.7 31.6 %while.27 = (s32[]{:T(128)}, f32[8,16,128]{2,1,0:T(8,128)S(1)}, s32[8]{0:T(128)S(1)}, f32[128,128]{1,0:T(8,128)}, f32[3,128,128]{2,0,1:T(4,128)S(1)}, /*index=5*...) while((s32[]{:T(128)}, f32[8,16,128]{2,1,0:T(8,128)S(1)}, ...), condition=%wide.region_10.11_spmd.clone.clone, body=%wide.region_5.10_spmd.clone.clone.sunk | while | flops 39806980 | bytes 268635 | solution.py:75
  116.9 0.7 fusion.113
  120.9 0.7 fusion.113
  124.8 0.7 fusion.113
  128.8 0.7 fusion.113
  132.7 0.7 fusion.113
  136.7 0.7 fusion.113
  140.6 0.7 fusion.113
  144.6 0.7 fusion.113
  145.6 26.0 %while.28 = (s32[]{:T(128)}, f32[3,131]{1,0:T(4,128)S(1)}, f32[128,128]{1,0:T(8,128)}, f32[3,128,128]{2,0,1:T(4,128)S(1)}, f32[128,128]{1,0:T(8,128)S(1)}, /*ind...) while((s32[]{:T(128)}, f32[3,131]{1,0:T(4,128)S(1)}, ...), condition=%wide.region_15.16_spmd.clone.clone, body=%wide.region_14.15_spmd.clone.clone.sunk | while | flops 39802800 | bytes 358733 | solution.py:107
  145.7 0.7 fusion.118
  146.4 0.6 fusion.119
  147.0 0.6 fusion.120
  147.6 0.6 fusion.121
  148.2 0.6 fusion.122
  148.9 0.7 fusion.118
  149.6 0.6 fusion.119
  150.3 0.6 fusion.120
  150.9 0.6 fusion.121
  151.5 0.6 fusion.122
  152.2 0.7 fusion.118
  152.9 0.6 fusion.119
  153.5 0.6 fusion.120
  154.1 0.6 fusion.121
  154.7 0.6 fusion.122
  155.4 0.7 fusion.118
  156.2 0.6 fusion.119
  156.8 0.6 fusion.120
  157.4 0.6 fusion.121
  158.0 0.6 fusion.122
  158.7 0.7 fusion.118
  160.0 0.6 fusion.120
  160.6 0.6 fusion.121
  161.3 0.6 fusion.122
  162.0 0.7 fusion.118
  163.3 0.6 fusion.120
  163.9 0.6 fusion.121
  164.5 0.6 fusion.122
  165.2 0.7 fusion.118
  166.5 0.6 fusion.120
  167.1 0.6 fusion.121
  167.8 0.6 fusion.122
  168.5 0.7 fusion.118
  169.8 0.6 fusion.120
  170.4 0.6 fusion.121
  171.0 0.6 fusion.122
  171.8 0.6 multiply_reduce_fusion.2
  172.4 2.2 collective-permute-start.1
  174.6 85.9 %scatter_custom_fusion = f32[32768]{0:T(1024)S(1)} fusion(s32[16384]{0:T(1024)S(1)} %fusion.84, f32[16384]{0:T(1024)S(1)} %get-tuple-element.350, f32[]{:T(128)} %constant.148.clone.1), kind=kCustom, calls=%fused_computation.114 | custom fusion | flops 16384 | bytes 131076 | tf_op jit(solution)/shard_map/scatter-add | solution.py:87
  260.5 0.7 reshape.50
  261.2 41.9 %all-reduce.1 = (f32[]{:T(128)}, f32[]{:T(128)}) all-reduce(f32[]{:T(128)S(6)} %add.198, f32[]{:T(128)} %multiply_reduce_fusion.2), channel_id=1, replica_groups=mesh['tm'=8,'cal'=4] {'tm','cal'}, use_global_device_ids=true, to_apply=%region_3.0 | all-reduce | flops 2 | bytes 16 | tf_op jit(solution)/shard_map/psum | solution.py:110
  305.1 0.7 multiply_reduce_fusion.7
  307.1 0.9 constant_dynamic-slice_fusion.3
  308.0 30.1 %psum.30 = f32[2,4096]{1,0:T(2,128)S(1)} all-reduce(f32[2,4096]{1,0:T(2,128)S(1)} %constant_dynamic-slice_fusion.3), channel_id=1, replica_groups=mesh['tm'=8,'cal'=4] {'tm'}, use_global_device_ids=true, to_apply=%region_18.19 | all-reduce | flops 8192 | bytes 65536 | tf_op jit(solution)/shard_map/psum | solution.py:112
  338.1 0.6 multiply_reduce_fusion.3
  339.4 46.4 %psum.31 = f32[]{:T(128)} all-reduce(f32[]{:T(128)S(6)} %add.207), channel_id=1, replica_groups=mesh['tm'=8,'cal'=4] {'tm','cal'}, use_global_device_ids=true, to_apply=%region_22.23 | all-reduce | flops 1 | bytes 8 | tf_op jit(solution)/shard_map/psum | solution.py:122
  388.4 0.6 multiply_add_fusion.1
  (135 shorter events, 27.7 us)
Async XLA Ops:
  7.2 3.9 copy-start.4
  7.2 299.9 %all-reduce.4.cloned.1.call-start = ((), (), s32[]{:S(2)}) async-start(), calls=%async_computation | async-start | bytes 262144
  7.2 106.4 %collective-permute-start = (f32[3,3]{1,0:T(4,128)}, f32[3,3]{1,0:T(4,128)S(1)}, u32[]{:S(2)}, u32[]{:S(2)}) collective-permute-start(f32[3,3]{1,0:T(4,128)} %bitcast.110), channel_id=1, source_target_pairs={{1,0},{2,1},{3,2},{4,3},{5,4},{6,5},{7,6},{8,7},{9,8},{10,9},{11,1... | collective-permute-start | bytes 116 | tf_op jit(solution)/shard_map/ppermute | solution.py:11
  10.1 6.4 %copy-start.3 = (f32[3,128,128]{2,1,0:T(8,128)S(1)}, f32[3,128,128]{2,1,0:T(8,128)}, u32[]{:S(2)}) copy-start(f32[3,128,128]{2,1,0:T(8,128)} %param.20) | copy-start | bytes 589828
  16.5 0.7 copy-start.12
  16.5 1.3 copy-start.13
  16.5 1.9 copy-start.6
  19.0 90.5 %copy-start = (f32[5,128,128]{2,1,0:T(8,128)S(1)}, f32[5,128,128]{2,1,0:T(8,128)}, u32[]{:S(2)}) copy-start(f32[5,128,128]{2,1,0:T(8,128)} %param.19) | copy-start | bytes 983044
  19.0 90.5 %copy-start.10 = (f32[5,128]{1,0:T(8,128)S(1)}, f32[5,128]{1,0:T(8,128)}, u32[]{:S(2)}) copy-start(f32[5,128]{1,0:T(8,128)} %param.31) | copy-start | bytes 7684
  109.5 0.8 copy-start.9
  109.6 2.8 copy-start.17
  109.6 4.0 %copy-start.14 = (f32[3,128]{1,0:T(4,128)S(1)}, f32[3,128]{1,0:T(4,128)}, u32[]{:S(2)}) copy-start(f32[3,128]{1,0:T(4,128)} %param.32) | copy-start | bytes 4612
  113.6 31.7 %copy-start.1 = (s32[128,128]{1,0:T(8,128)S(1)}, s32[128,128]{1,0:T(8,128)}, u32[]{:S(2)}) copy-start(s32[128,128]{1,0:T(8,128)} %param.26) | copy-start | bytes 196612
  113.6 31.7 %copy-start.2 = (s32[128,128]{1,0:T(8,128)S(1)}, s32[128,128]{1,0:T(8,128)}, u32[]{:S(2)}) copy-start(s32[128,128]{1,0:T(8,128)} %param.25) | copy-start | bytes 196612
  113.7 31.7 %copy-start.7 = (f32[128,128]{1,0:T(8,128)S(1)}, f32[128,128]{1,0:T(8,128)}, u32[]{:S(2)}) copy-start(f32[128,128]{1,0:T(8,128)} %param.22) | copy-start | bytes 196612
  113.7 31.7 %copy-start.8 = (f32[128,128]{1,0:T(8,128)S(1)}, f32[128,128]{1,0:T(8,128)}, u32[]{:S(2)}) copy-start(f32[128,128]{1,0:T(8,128)} %param.23) | copy-start | bytes 196612
  113.7 31.7 %copy-start.16 = (s32[128]{0:T(128)S(1)}, s32[128]{0:T(128)}, u32[]{:S(2)}) copy-start(s32[128]{0:T(128)} %param.27) | copy-start | bytes 1540
  172.4 132.7 %collective-permute-start.1 = (f32[3,3]{1,0:T(4,128)S(1)}, f32[3,3]{1,0:T(4,128)S(1)}, u32[]{:S(2)}, u32[]{:S(2)}) collective-permute-start(f32[3,3]{1,0:T(4,128)S(1)} %slice.14), channel_id=1, source_target_pairs={{0,1},{1,2},{2,3},{3,4},{4,5},{5,6},{6,7},{7,8},{8,9},{9,10},{10,1... | collective-permute-start | bytes 116 | tf_op jit(solution)/shard_map/ppermute | solution.py:11
  305.0 84.0 %copy-start.11 = (f32[5,128]{1,0:T(8,128)}, f32[5,128]{1,0:T(8,128)S(1)}, u32[]{:S(2)}) copy-start(f32[5,128]{1,0:T(8,128)S(1)} %get-tuple-element.349) | copy-start | bytes 7684
  305.7 83.3 %copy-start.15 = (f32[3,128]{1,0:T(4,128)}, f32[3,128]{1,0:T(4,128)S(1)}, u32[]{:S(2)}) copy-start(f32[3,128]{1,0:T(4,128)S(1)} %get-tuple-element.347) | copy-start | bytes 4612
  338.8 50.2 %copy-start.5 = (f32[2,4096]{1,0:T(2,128)}, f32[2,4096]{1,0:T(2,128)S(1)}, u32[]{:S(2)}) copy-start(f32[2,4096]{1,0:T(2,128)S(1)} %get-tuple-element.345) | copy-start | bytes 98308
Sparse Core Ops, SparseCore 0:
  261.3 33.1 all-reduce.3
where the time goes:
time: 398 us; the launch traced here: 396 us
  blocking collectives  124 us (31%)
  other arithmetic  106 us (27%)
  local copies, waits for them, and re-layouts  98.9 us (25%)
  matrix products  35.3 us (9%)
  between operations  21.6 us (5%)
  loops' own time  6.01 us (2%)
  starting transfers between devices  4.2 us (1%)
    gather x1, local copies, waits for them, and re-layouts, local(): y_cal = cal_design * jnp.take(cal_values.reshape(-1), flat_index)  90.5 us
    scatter-add x1, other arithmetic, local(): jax.ops.segment_sum((cal_design * weighted).reshape(-1), flat_index.resha...  85.9 us
    psum x1, blocking collectives, local(): norm_next = lax.psum(next_local, ('tm', 'cal'))  46.4 us
    psum x1, blocking collectives, local(): norm_now, curvature = lax.psum((norm_local, curv_local), ('tm', 'cal'))  41.9 us
    psum x1, blocking collectives, local(): q_cal = lax.psum(shared, 'tm')  30.1 us
    dot_general x32, matrix products, backward(): jnp.einsum('cbo,bok->ck', weights[offset][None] * scaled, onehot, precisi...  19.8 us
    dot_general x32, matrix products, forward(): jnp.einsum('bok,ck->cbo', onehot, att_ext, precision=lax.Precision.HIGHEST)  15.4 us
  transfers between devices with their start and end apart: 3, of which 0 were waited for; matrix products, arithmetic and copies ran while one was open for 46% of the time, Pallas kernels for 0%

commit v1 on v0

--- a/solution.py
+++ b/solution.py
@@ -119,7 +119,7 @@
         + jnp.sum(new_att_res * new_att_res)
         + first_row * jnp.sum(new_cal_res * new_cal_res)
     )
-    norm_next = lax.psum(next_local, ("tm", "cal"))
+    norm_next = lax.psum(lax.psum(next_local, "cal"), "tm")
     ratio = norm_next / norm_now
     return (
         new_src_res,

time: 398 us -> 383 us (0.962)
  blocking collectives: 124 us -> 106 us
    psum x1 -> x2, blocking collectives: 46.4 us -> 29 us  [local(): norm_next = lax.psum(lax.psum(next_local, 'cal'), 'tm')]
  transfers between devices with their start and end apart: 3 -> 3, of which waited for: 0 -> 0; matrix products, arithmetic and copies ran while one was open for 46% -> 48% of each run, Pallas kernels for 0% -> 0%
where the time goes in v1:
time: 383 us; the launch traced here: 378 us
  other arithmetic  106 us (28%)
  blocking collectives  106 us (28%)
  local copies, waits for them, and re-layouts  98.9 us (26%)
  matrix products  35.3 us (9%)
  between operations  21.6 us (6%)
  loops' own time  6.01 us (2%)
  starting transfers between devices  4.2 us (1%)
    gather x1, local copies, waits for them, and re-layouts, local(): y_cal = cal_design * jnp.take(cal_values.reshape(-1), flat_index)  90.5 us
    scatter-add x1, other arithmetic, local(): jax.ops.segment_sum((cal_design * weighted).reshape(-1), flat_index.resha...  85.9 us
    psum x1, blocking collectives, local(): norm_now, curvature = lax.psum((norm_local, curv_local), ('tm', 'cal'))  41.9 us
    psum x1, blocking collectives, local(): q_cal = lax.psum(shared, 'tm')  30.1 us
    psum x2, blocking collectives, local(): norm_next = lax.psum(lax.psum(next_local, 'cal'), 'tm')  29 us
    dot_general x32, matrix products, backward(): jnp.einsum('cbo,bok->ck', weights[offset][None] * scaled, onehot, precisi...  19.8 us
    dot_general x32, matrix products, forward(): jnp.einsum('bok,ck->cbo', onehot, att_ext, precision=lax.Precision.HIGHEST)  15.4 us
  transfers between devices with their start and end apart: 3, of which 0 were waited for; matrix products, arithmetic and copies ran while one was open for 48% of the time, Pallas kernels for 0%

profile of v1, /device:TPU:14, one launch (start us, length us, event | category | flops | bytes accessed | tf_op | source)
XLA Modules:
  0.0 378.4 jit_solution(2400577012744551419)
XLA Ops:
  7.2 1.9 collective-permute-start
  9.2 0.9 bitcast_clamp_fusion
  10.1 0.9 fusion.84
  11.0 5.4 %all-gather = f32[4,2,4096]{2,1,0:T(2,128)S(1)} all-gather(f32[1,2,4096]{2,1,0:T(2,128)S(1)} %bitcast.109), channel_id=1, replica_groups=mesh['tm'=8,'cal'=4] {'cal'}, dimensions={0}, use_global_device_ids=true | all-gather | bytes 163840 | tf_op jit(solution)/shard_map/all_gather | solution.py:50
  18.3 0.6 multiply_reduce_fusion.4
  19.0 90.5 %gather_fusion = f32[16384]{0:T(1024)S(1)} fusion(f32[32768]{0:T(1024)S(1)} %bitcast.107, s32[16384]{0:T(1024)S(1)} %bitcast_clamp_fusion), kind=kCustom, calls=%fused_computation | custom fusion | bytes 196608 | tf_op jit(solution)/shard_map/jit(_take)/gather | solution.py:78
  109.7 0.6 copy-done.9
  113.7 31.6 %while.27 = (s32[]{:T(128)}, f32[8,16,128]{2,1,0:T(8,128)S(1)}, s32[8]{0:T(128)S(1)}, f32[128,128]{1,0:T(8,128)}, f32[3,128,128]{2,0,1:T(4,128)S(1)}, /*index=5*...) while((s32[]{:T(128)}, f32[8,16,128]{2,1,0:T(8,128)S(1)}, ...), condition=%wide.region_10.11_spmd.clone.clone, body=%wide.region_5.10_spmd.clone.clone.sunk | while | flops 39806980 | bytes 268635 | solution.py:75
  116.9 0.7 fusion.113
  120.9 0.7 fusion.113
  124.8 0.7 fusion.113
  128.8 0.7 fusion.113
  132.7 0.7 fusion.113
  136.7 0.7 fusion.113
  140.6 0.7 fusion.113
  144.6 0.7 fusion.113
  145.6 26.0 %while.28 = (s32[]{:T(128)}, f32[3,131]{1,0:T(4,128)S(1)}, f32[128,128]{1,0:T(8,128)}, f32[3,128,128]{2,0,1:T(4,128)S(1)}, f32[128,128]{1,0:T(8,128)S(1)}, /*ind...) while((s32[]{:T(128)}, f32[3,131]{1,0:T(4,128)S(1)}, ...), condition=%wide.region_15.16_spmd.clone.clone, body=%wide.region_14.15_spmd.clone.clone.sunk | while | flops 39802800 | bytes 358733 | solution.py:107
  145.7 0.7 fusion.118
  146.4 0.6 fusion.119
  147.0 0.6 fusion.120
  147.6 0.6 fusion.121
  148.2 0.6 fusion.122
  148.9 0.7 fusion.118
  149.6 0.6 fusion.119
  150.3 0.6 fusion.120
  150.9 0.6 fusion.121
  151.5 0.6 fusion.122
  152.2 0.7 fusion.118
  153.5 0.6 fusion.120
  154.1 0.6 fusion.121
  154.7 0.6 fusion.122
  155.4 0.7 fusion.118
  156.2 0.6 fusion.119
  156.8 0.6 fusion.120
  157.4 0.6 fusion.121
  158.0 0.6 fusion.122
  158.7 0.7 fusion.118
  160.0 0.6 fusion.120
  160.6 0.6 fusion.121
  161.3 0.6 fusion.122
  162.0 0.7 fusion.118
  163.3 0.6 fusion.120
  163.9 0.6 fusion.121
  164.5 0.6 fusion.122
  165.2 0.7 fusion.118
  166.5 0.6 fusion.120
  167.1 0.6 fusion.121
  167.8 0.6 fusion.122
  168.5 0.7 fusion.118
  169.8 0.6 fusion.120
  170.4 0.6 fusion.121
  171.0 0.6 fusion.122
  171.8 0.6 multiply_reduce_fusion.2
  172.4 2.2 collective-permute-start.1
  174.6 85.9 %scatter_custom_fusion = f32[32768]{0:T(1024)S(1)} fusion(s32[16384]{0:T(1024)S(1)} %fusion.84, f32[16384]{0:T(1024)S(1)} %get-tuple-element.350, f32[]{:T(128)} %constant.148.clone.1), kind=kCustom, calls=%fused_computation.114 | custom fusion | flops 16384 | bytes 131076 | tf_op jit(solution)/shard_map/scatter-add | solution.py:87
  260.5 0.7 reshape.50
  261.2 41.9 %all-reduce.1 = (f32[]{:T(128)}, f32[]{:T(128)}) all-reduce(f32[]{:T(128)S(6)} %add.200, f32[]{:T(128)} %multiply_reduce_fusion.2), channel_id=1, replica_groups=mesh['tm'=8,'cal'=4] {'tm','cal'}, use_global_device_ids=true, to_apply=%region_3.0 | all-reduce | flops 2 | bytes 16 | tf_op jit(solution)/shard_map/psum | solution.py:110
  305.1 0.7 multiply_reduce_fusion.7
  307.1 0.9 constant_dynamic-slice_fusion.3
  308.0 30.1 %psum.37 = f32[2,4096]{1,0:T(2,128)S(1)} all-reduce(f32[2,4096]{1,0:T(2,128)S(1)} %constant_dynamic-slice_fusion.3), channel_id=1, replica_groups=mesh['tm'=8,'cal'=4] {'tm'}, use_global_device_ids=true, to_apply=%region_18.19 | all-reduce | flops 8192 | bytes 65536 | tf_op jit(solution)/shard_map/psum | solution.py:112
  338.1 0.6 multiply_reduce_fusion.3
  339.4 6.3 %psum.38 = f32[]{:T(128)} all-reduce(f32[]{:T(128)S(6)} %add.209), channel_id=1, replica_groups=mesh['tm'=8,'cal'=4] {'cal'}, use_global_device_ids=true, to_apply=%region_22.23 | all-reduce | flops 1 | bytes 8 | tf_op jit(solution)/shard_map/psum | solution.py:122
  345.7 22.7 %psum.39 = f32[]{:T(128)} all-reduce(f32[]{:T(128)} %psum.38), channel_id=1, replica_groups=mesh['tm'=8,'cal'=4] {'tm'}, use_global_device_ids=true, to_apply=%region_23.24 | all-reduce | flops 1 | bytes 8 | tf_op jit(solution)/shard_map/psum | solution.py:122
  370.9 0.6 multiply_add_fusion.1
  (136 shorter events, 28.3 us)
Async XLA Ops:
  7.2 3.9 %copy-start.4 = (f32[2,4096]{1,0:T(2,128)S(1)}, f32[2,4096]{1,0:T(2,128)}, u32[]{:S(2)}) copy-start(f32[2,4096]{1,0:T(2,128)} %param.33) | copy-start | bytes 98308
  7.2 299.9 %all-reduce.4.cloned.1.call-start = ((), (), s32[]{:S(2)}) async-start(), calls=%async_computation | async-start | bytes 262144
  7.2 106.4 %collective-permute-start = (f32[3,3]{1,0:T(4,128)}, f32[3,3]{1,0:T(4,128)S(1)}, u32[]{:S(2)}, u32[]{:S(2)}) collective-permute-start(f32[3,3]{1,0:T(4,128)} %bitcast.110), channel_id=1, source_target_pairs={{1,0},{2,1},{3,2},{4,3},{5,4},{6,5},{7,6},{8,7},{9,8},{10,9},{11,1... | collective-permute-start | bytes 116 | tf_op jit(solution)/shard_map/ppermute | solution.py:11
  10.1 6.4 %copy-start.3 = (f32[3,128,128]{2,1,0:T(8,128)S(1)}, f32[3,128,128]{2,1,0:T(8,128)}, u32[]{:S(2)}) copy-start(f32[3,128,128]{2,1,0:T(8,128)} %param.20) | copy-start | bytes 589828
  16.5 0.7 copy-start.12
  16.5 1.3 copy-start.13
  16.5 1.9 copy-start.6
  19.0 90.5 %copy-start = (f32[5,128,128]{2,1,0:T(8,128)S(1)}, f32[5,128,128]{2,1,0:T(8,128)}, u32[]{:S(2)}) copy-start(f32[5,128,128]{2,1,0:T(8,128)} %param.19) | copy-start | bytes 983044
  19.0 90.5 %copy-start.10 = (f32[5,128]{1,0:T(8,128)S(1)}, f32[5,128]{1,0:T(8,128)}, u32[]{:S(2)}) copy-start(f32[5,128]{1,0:T(8,128)} %param.31) | copy-start | bytes 7684
  109.5 0.8 copy-start.9
  109.6 2.8 copy-start.17
  109.6 4.0 %copy-start.14 = (f32[3,128]{1,0:T(4,128)S(1)}, f32[3,128]{1,0:T(4,128)}, u32[]{:S(2)}) copy-start(f32[3,128]{1,0:T(4,128)} %param.32) | copy-start | bytes 4612
  113.6 31.7 %copy-start.1 = (s32[128,128]{1,0:T(8,128)S(1)}, s32[128,128]{1,0:T(8,128)}, u32[]{:S(2)}) copy-start(s32[128,128]{1,0:T(8,128)} %param.26) | copy-start | bytes 196612
  113.6 31.7 %copy-start.2 = (s32[128,128]{1,0:T(8,128)S(1)}, s32[128,128]{1,0:T(8,128)}, u32[]{:S(2)}) copy-start(s32[128,128]{1,0:T(8,128)} %param.25) | copy-start | bytes 196612
  113.7 31.7 %copy-start.7 = (f32[128,128]{1,0:T(8,128)S(1)}, f32[128,128]{1,0:T(8,128)}, u32[]{:S(2)}) copy-start(f32[128,128]{1,0:T(8,128)} %param.22) | copy-start | bytes 196612
  113.7 31.7 %copy-start.8 = (f32[128,128]{1,0:T(8,128)S(1)}, f32[128,128]{1,0:T(8,128)}, u32[]{:S(2)}) copy-start(f32[128,128]{1,0:T(8,128)} %param.23) | copy-start | bytes 196612
  113.7 31.7 %copy-start.16 = (s32[128]{0:T(128)S(1)}, s32[128]{0:T(128)}, u32[]{:S(2)}) copy-start(s32[128]{0:T(128)} %param.27) | copy-start | bytes 1540
  172.4 132.7 %collective-permute-start.1 = (f32[3,3]{1,0:T(4,128)S(1)}, f32[3,3]{1,0:T(4,128)S(1)}, u32[]{:S(2)}, u32[]{:S(2)}) collective-permute-start(f32[3,3]{1,0:T(4,128)S(1)} %slice.14), channel_id=1, source_target_pairs={{0,1},{1,2},{2,3},{3,4},{4,5},{5,6},{6,7},{7,8},{8,9},{9,10},{10,1... | collective-permute-start | bytes 116 | tf_op jit(solution)/shard_map/ppermute | solution.py:11
  305.0 66.5 %copy-start.11 = (f32[5,128]{1,0:T(8,128)}, f32[5,128]{1,0:T(8,128)S(1)}, u32[]{:S(2)}) copy-start(f32[5,128]{1,0:T(8,128)S(1)} %get-tuple-element.349) | copy-start | bytes 7684
  305.7 65.8 %copy-start.15 = (f32[3,128]{1,0:T(4,128)}, f32[3,128]{1,0:T(4,128)S(1)}, u32[]{:S(2)}) copy-start(f32[3,128]{1,0:T(4,128)S(1)} %get-tuple-element.347) | copy-start | bytes 4612
  338.8 32.8 %copy-start.5 = (f32[2,4096]{1,0:T(2,128)}, f32[2,4096]{1,0:T(2,128)S(1)}, u32[]{:S(2)}) copy-start(f32[2,4096]{1,0:T(2,128)S(1)} %get-tuple-element.345) | copy-start | bytes 98308
Sparse Core Ops, SparseCore 0:
  261.3 33.1 all-reduce.3
